TPU v7x, 256 devices: a whole 4x4x8 slice. The times are simulated.
256 devices in a mesh: pipe: 2 (over core), seq: 4 (over x), tensor: 32 (over z, y).
Axes of the slice: x: 4, y: 4, z: 8, core: 2. Of those that a mesh axis runs over, the one named last changes fastest.
Arguments:
- token_ids: int32 [2, 768], P(None, 'seq'), may hold values from 0 to 511
- embed_table: bfloat16 [512, 8192], P(None, 'tensor'), may hold values from -24 to 24
- in_proj: bfloat16 [2, 8192, 3, 4096], P('pipe', None, None, 'tensor'), may hold values from -0.0625 to 0.0625
- feat_taps: float32 [2, 3, 3, 4096], P('pipe', None, None, 'tensor'), may hold values from -3 to 3
- se_taps: float32 [7, 4096], P(None, 'tensor'), may hold values from -2 to 2
- mr_taps: float32 [128, 4096], P(None, 'tensor'), may hold values from -0.6 to 0.6
- out_proj: bfloat16 [2, 4096, 8192], P('pipe', 'tensor'), may hold values from -0.1875 to 0.1875
- norm_gain: bfloat16 [2, 8192], P('pipe', 'tensor'), may hold values from 0.25 to 1.75
Outputs:
- segment_out: bfloat16 [2, 2, 768, 8192], P('pipe', None, 'seq', 'tensor')
All inputs are finite; a program needn't handle non-finite values.
Results may differ from a plain program's by a relative error of at most 0.023.
Values may be sent and summed in bfloat16 or wider, within the bound.
No kernel may reach another device: no remote copies, remote signals or barrier semaphores. Data moves between devices by JAX's collectives and lax.ppermute only.
A program may use at most 64 MiB of HBM per device.

v0:
```python
import jax
import jax.numpy as jnp
from jax import lax
from jax.sharding import PartitionSpec as P

VOCAB = 512
KL = 128
KS = 7
KF = 3
SEGMENTS = 2
HALO = 129
epsilon = 1e-06


def from_behind(value, axis, steps):
    count = lax.axis_size(axis)
    pairs = [(source, (source + steps) % count) for source in range(count)]
    return lax.ppermute(value, axis, pairs)


def passed_along(value, axis, steps):
    count = lax.axis_size(axis)
    first, last = (max(0, -steps), min(count, count - steps))
    return lax.ppermute(value, axis, [(source, source + steps) for source in range(first, last)])


def project(stream, w_flat, gain_cols):
    gathered, gain_all = (
        lax.all_gather(stream, "tensor", axis=2, tiled=True),
        lax.all_gather(gain_cols, "tensor", axis=1, tiled=True),
    )
    values = gathered.astype(jnp.float32)
    inv_rms = lax.rsqrt(jnp.mean(values * values, axis=2, keepdims=True) + epsilon)
    normed = (values * inv_rms * gain_all[0].astype(jnp.float32)).astype(jnp.bfloat16)
    projected = jnp.einsum("snd,dk->snk", normed, w_flat, preferred_element_type=jnp.float32)
    return projected.astype(jnp.bfloat16)


def send_tails(projected):
    row_count = projected.shape[1]
    chan_local = projected.shape[2] // 3
    kv_tail = projected[:, row_count - HALO :, chan_local:]
    q_tail = projected[:, row_count - (KF - 1) :, :chan_local]
    return from_behind((kv_tail, q_tail), "seq", 1)


def hand_over(result):
    return passed_along(result, "pipe", 1)


def mixing(stream, projected, kv_prev, q_prev, feat_local, long_taps, w_down):
    row_count = projected.shape[1]
    chan_local = projected.shape[2] // 3
    q_all = jnp.concatenate([q_prev, projected[:, :, :chan_local]], axis=1).astype(jnp.float32)
    kv_all = jnp.concatenate([kv_prev, projected[:, :, chan_local:]], axis=1).astype(jnp.float32)
    q_taps = feat_local[0, :, 0, :]
    kv_taps = feat_local[0, :, 1:, :].reshape(KF, 2 * chan_local)
    kv_span = KL - 1 + row_count
    q_feat = jnp.zeros((projected.shape[0], row_count, chan_local), jnp.float32)
    kv_feat = jnp.zeros((projected.shape[0], kv_span, 2 * chan_local), jnp.float32)
    for tap_index in range(KF):
        offset = KF - 1 - tap_index
        q_feat = q_feat + q_taps[tap_index] * q_all[:, offset : offset + row_count]
        kv_feat = kv_feat + kv_taps[tap_index] * kv_all[:, offset : offset + kv_span]
    gated_kv = kv_feat[:, :, :chan_local] * kv_feat[:, :, chan_local:]

    def add_tap(tap_index, running):
        shifted = lax.dynamic_slice_in_dim(gated_kv, KL - 1 - tap_index, row_count, 1)
        return running + long_taps[tap_index] * shifted

    filtered = lax.fori_loop(0, KL, add_tap, jnp.zeros_like(q_feat))
    y_out = (q_feat * filtered).astype(jnp.bfloat16)
    partial_terms = jnp.einsum("snc,cd->snd", y_out, w_down[0], preferred_element_type=jnp.float32)
    mixed = lax.psum_scatter(
        partial_terms.astype(jnp.bfloat16), "tensor", scatter_dimension=2, tiled=True
    ).astype(jnp.float32)
    return (stream.astype(jnp.float32) + mixed).astype(jnp.bfloat16)


def local(token_ids, embed_table, in_proj, feat_taps, se_taps, mr_taps, out_proj, norm_gain):
    section = lax.axis_index("pipe")
    shard_pos = lax.axis_index("seq")
    lead_segment = section == 0
    padded_se = jnp.concatenate(
        [se_taps, jnp.zeros((KL - KS, se_taps.shape[1]), jnp.float32)], axis=0
    )
    long_taps = jnp.where(lead_segment, padded_se, mr_taps)
    w_flat = in_proj[0].reshape(in_proj.shape[1], -1)
    vocab_ids = jnp.arange(VOCAB, dtype=jnp.int32)
    one_hot = (token_ids[:, :, None] == vocab_ids[None, None, :]).astype(jnp.bfloat16)
    embedded = jnp.einsum(
        "snv,vd->snd", one_hot, embed_table, preferred_element_type=jnp.float32
    ).astype(jnp.bfloat16)
    current = jnp.where(lead_segment, embedded, jnp.zeros_like(embedded))
    outputs = []
    for step_index in range(SEGMENTS):
        projected = project(current, w_flat, norm_gain)
        kv_recv, q_recv = send_tails(projected)
        kv_earlier = jnp.concatenate([jnp.zeros_like(kv_recv[:1]), kv_recv[:-1]], axis=0)
        q_earlier = jnp.concatenate([jnp.zeros_like(q_recv[:1]), q_recv[:-1]], axis=0)
        kv_prev = jnp.where(shard_pos == 0, kv_earlier, kv_recv)
        q_prev = jnp.where(shard_pos == 0, q_earlier, q_recv)
        result = mixing(current, projected, kv_prev, q_prev, feat_taps, long_taps, out_proj)
        outputs.append(result)
        if step_index + 1 < SEGMENTS:
            current = hand_over(result)
    final_out = lax.dynamic_index_in_dim(jnp.stack(outputs, axis=0), section, 0, keepdims=True)
    return final_out


def solution(mesh):
    return jax.shard_map(
        local,
        mesh=mesh,
        in_specs=(
            P(None, "seq"),
            P(None, "tensor"),
            P("pipe", None, None, "tensor"),
            P("pipe", None, None, "tensor"),
            P(None, "tensor"),
            P(None, "tensor"),
            P("pipe", "tensor", None),
            P("pipe", "tensor"),
        ),
        out_specs=P("pipe", None, "seq", "tensor"),
        check_vma=False,
    )
```

profile of v0, /device:TPU:4, one launch (start us, length us, event | category | flops | bytes accessed | tf_op | source)
XLA Modules:
  0.0 731.5 jit_solution(4473578818724126440)
XLA Ops:
  6.5 2.1 fusion.22
  8.8 8.7 %copy.9 = bf16[1,8192,3,128]{1,3,2,0:T(8,128)(2,1)} copy(bf16[1,8192,3,128]{3,1,2,0:T(8,128)(2,1)} %param.14) | data formatting | bytes 12582912 | tf_op args[2]
  17.5 46.2 %all_gather.11 = bf16[1,8192]{1,0:T(2,128)(2,1)S(1)} all-gather(bf16[1,256]{1,0:T(2,128)(2,1)S(1)} %copy-done.9), channel_id=1, replica_groups=mesh['pipe'=2,'seq'=4,'tensor'=32] {'tensor'}, dimensions={1}, use_global_device_ids=true | all-gather | bytes 16896 | tf_op jit(solution)/shard_map/all_gather | solution.py:30
  63.8 41.7 %all-gather.3.cloned.1.call-done = bf16[2,192,8192]{2,1,0:T(8,128)(2,1)} async-done(((bf16[2,192,256]{2,1,0:T(8,128)(2,1)}), bf16[2,192,8192]{2,1,0:T(8,128)(2,1)}) %all-gather.3.cloned.1.call-update) | async-done | bytes 6291472 | tf_op jit(solution)/shard_map/all_gather | solution.py:29
  105.5 4.3 fusion
  109.8 0.3 copy-done.1
  110.1 5.8 fusion.16
  115.9 1.2 collective-permute-start
  117.3 0.7 collective-permute-start.1
  117.9 1.7 collective-permute-done
  119.6 2.8 collective-permute-done.1
  122.7 16.4 %while.32 = (s32[]{:T(128)}, f32[2,192,128]{2,1,0:T(8,128)S(1)}, f32[128,128]{1,0:T(8,128)S(1)}, f32[2,319,128]{2,1,0:T(8,128)S(1)}, s32[]{:T(128)}, /*index=5*/s32[]{:T(128)}, s32[]{:T(128)}, s32[]{:T(128)}) while((s32[]{:T(128)}, f32[2,192,128]{2,1,0:T(8,128)S(1)}, f32[128,128]{1,0:T(8,128)S(1)}, f32[2,319,128]{2,1,0:T(8,128)S(1)}, ...), condition=%wide.region_2.3_spmd.clone, body=%wide.region_1.2_spmd.clone.sunk | while | flops 147463 | bytes 591509 | solution.py:71
  139.2 4.4 convolution_convert_fusion.1
  143.7 223.0 %reduce-scatter.3.cloned.1.call-done = bf16[2,192,256]{2,1,0:T(8,128)(2,1)} async-done(((bf16[2,192,8192]{2,1,0:T(8,128)(2,1)}), bf16[2,192,256]{2,1,0:T(8,128)(2,1)}) %reduce-scatter.3.cloned.1.call-update) | async-done | bytes 196624 | tf_op jit(solution)/shard_map/reduce_scatter | solution.py:74
  366.7 1.0 add_convert_fusion.1
  367.7 1.3 collective-permute-start.2
  369.0 1.0 collective-permute-done.2
  370.0 0.7 copy-done.4
  370.7 0.2 reduce-scatter.5.cloned.1.call-start
  370.9 90.8 %all-gather.5.cloned.1.call-done = bf16[2,192,8192]{2,1,0:T(8,128)(2,1)} async-done(((bf16[2,192,256]{2,1,0:T(8,128)(2,1)}), bf16[2,192,8192]{2,1,0:T(8,128)(2,1)}) %all-gather.5.cloned.1.call-update) | async-done | bytes 6291472 | tf_op jit(solution)/shard_map/all_gather | solution.py:29
  461.8 4.3 fusion.3
  466.0 0.3 copy-done.2
  466.4 6.2 fusion.19
  472.6 1.3 collective-permute-start.3
  474.0 0.6 collective-permute-start.4
  474.6 1.7 collective-permute-done.3
  476.3 2.8 collective-permute-done.4
  479.5 16.4 %while.33 = (s32[]{:T(128)}, f32[2,192,128]{2,1,0:T(8,128)S(1)}, f32[128,128]{1,0:T(8,128)S(1)}, f32[2,319,128]{2,1,0:T(8,128)S(1)}, s32[]{:T(128)}, /*index=5*/s32[]{:T(128)}, s32[]{:T(128)}, s32[]{:T(128)}) while((s32[]{:T(128)}, f32[2,192,128]{2,1,0:T(8,128)S(1)}, f32[128,128]{1,0:T(8,128)S(1)}, f32[2,319,128]{2,1,0:T(8,128)S(1)}, ...), condition=%wide.region_6.7_spmd.clone, body=%wide.region_5.6_spmd.clone.sunk | while | flops 147463 | bytes 591509 | solution.py:71
  495.9 4.5 convolution_convert_fusion
  500.4 222.8 %reduce-scatter.5.cloned.1.call-done = bf16[2,192,256]{2,1,0:T(8,128)(2,1)} async-done(((bf16[2,192,8192]{2,1,0:T(8,128)(2,1)}), bf16[2,192,256]{2,1,0:T(8,128)(2,1)}) %reduce-scatter.5.cloned.1.call-update) | async-done | bytes 196624 | tf_op jit(solution)/shard_map/reduce_scatter | solution.py:74
  723.2 1.0 fusion.29
  724.2 0.8 fusion.30
  (568 shorter events, 24.4 us)
Async XLA Ops:
  6.5 132.6 %copy-start = (bf16[1,128,8192]{2,1,0:T(8,128)(2,1)S(1)}, bf16[1,128,8192]{2,1,0:T(8,128)(2,1)}, u32[]{:S(2)}) copy-start(bf16[1,128,8192]{2,1,0:T(8,128)(2,1)} %param.18) | copy-start | bytes 6291460
  6.5 99.0 %all-gather.3.cloned.1.call-start = ((), (), s32[]{:S(2)}) async-start(), calls=%async_computation.2 | async-start | bytes 6488064 | tf_op jit(solution)/shard_map/all_gather | solution.py:29
  8.7 8.8 %copy-start.9 = (bf16[1,256]{1,0:T(2,128)(2,1)S(1)}, bf16[1,256]{1,0:T(2,128)(2,1)}, u32[]{:S(2)}) copy-start(bf16[1,256]{1,0:T(2,128)(2,1)} %param.19) | copy-start | bytes 1540
  8.7 55.1 %copy-start.7 = (f32[1,3,3,128]{3,0,2,1:T(1,128)S(1)}, f32[1,3,3,128]{3,0,2,1:T(1,128)}, u32[]{:S(2)}) copy-start(f32[1,3,3,128]{3,0,2,1:T(1,128)} %param.15) | copy-start | bytes 13828
  8.7 55.1 %copy-start.6 = (f32[128,128]{1,0:T(8,128)S(1)}, f32[128,128]{1,0:T(8,128)}, u32[]{:S(2)}) copy-start(f32[128,128]{1,0:T(8,128)} %param.17) | copy-start | bytes 196612
  8.7 55.1 %copy-start.8 = (f32[7,128]{1,0:T(8,128)S(1)}, f32[7,128]{1,0:T(8,128)}, u32[]{:S(2)}) copy-start(f32[7,128]{1,0:T(8,128)} %param.16) | copy-start | bytes 10756
  8.7 358.0 %reduce-scatter.3.cloned.1.call-start = ((), (), s32[]{:S(2)}) async-start(), calls=%async_computation.3 | async-start | bytes 6488064 | tf_op jit(solution)/shard_map/reduce_scatter | solution.py:74
  105.5 4.6 copy-start.1
  115.9 3.6 collective-permute-start
  117.3 5.1 collective-permute-start.1
  139.2 227.5 %copy-start.3 = (bf16[2,192,256]{2,1,0:T(8,128)(2,1)S(1)}, bf16[2,192,256]{2,1,0:T(8,128)(2,1)}, u32[]{:S(2)}) copy-start(bf16[2,192,256]{2,1,0:T(8,128)(2,1)} %fusion.22) | copy-start | bytes 589828
  143.6 318.2 %all-gather.5.cloned.1.call-start = ((), (), s32[]{:S(2)}) async-start(), calls=%async_computation.4 | async-start | bytes 6488064 | tf_op jit(solution)/shard_map/all_gather | solution.py:29
  367.7 2.4 collective-permute-start.2
  370.0 0.7 copy-start.4
  370.7 352.5 %reduce-scatter.5.cloned.1.call-start = ((), (), s32[]{:S(2)}) async-start(), calls=%async_computation.5 | async-start | bytes 6488064 | tf_op jit(solution)/shard_map/reduce_scatter | solution.py:74
  461.8 4.6 copy-start.2
  472.6 3.6 collective-permute-start.3
  474.0 5.1 collective-permute-start.4
  495.9 227.3 %copy-start.5 = (bf16[2,192,256]{2,1,0:T(8,128)(2,1)S(1)}, bf16[2,192,256]{2,1,0:T(8,128)(2,1)}, u32[]{:S(2)}) copy-start(bf16[2,192,256]{2,1,0:T(8,128)(2,1)} %copy-done.4) | copy-start | bytes 589828
Sparse Core Ops, SparseCore 0:
  9.8 95.6 all-gather.2
  143.7 222.8 reduce-scatter.2
  370.8 90.9 all-gather.4
  500.5 222.6 reduce-scatter.4
where the time goes:
time: 732 us; the launch traced here: 731 us
  waiting for transfers between devices  588 us (80%)
  blocking collectives  46.2 us (6%)
  other arithmetic  32.8 us (4%)
  matrix products  23.1 us (3%)
  between operations  13.4 us (2%)
  local copies, waits for them, and re-layouts  12.7 us (2%)
  loops' own time  9.56 us (1%)
    reduce_scatter x2, waiting for transfers between devices, mixing(): lax.psum_scatter(partial_terms.astype(jnp.bfloat16), 'tensor', scatter_di...  446 us
    all_gather x2, waiting for transfers between devices, project(): lax.all_gather(stream, 'tensor', axis=2, tiled=True)  132 us
    all_gather x1, blocking collectives, project(): lax.all_gather(gain_cols, 'tensor', axis=1, tiled=True)  46.2 us
    add x256, other arithmetic, add_tap(): return running + long_taps[tap_index] * shifted  20.9 us
  transfers between devices with their start and end apart: 9, of which 9 were waited for; matrix products, arithmetic and copies ran while one was open for 1% of the time, Pallas kernels for 0%

commit v1 on v0

--- a/solution.py
+++ b/solution.py
@@ -10,6 +10,15 @@
 SEGMENTS = 2
 HALO = 129
 epsilon = 1e-06
+rates_supply_all = lambda field_in, chip_axis, dim_i: jnp.concatenate(
+    lax.all_to_all(
+        jnp.stack(lax.axis_size(chip_axis) * [field_in]),
+        axis_name=chip_axis,
+        split_axis=0,
+        concat_axis=0,
+    ),
+    axis=dim_i,
+)
 
 
 def from_behind(value, axis, steps):
@@ -26,7 +35,7 @@
 
 def project(stream, w_flat, gain_cols):
     gathered, gain_all = (
-        lax.all_gather(stream, "tensor", axis=2, tiled=True),
+        rates_supply_all(stream, "tensor", 2),
         lax.all_gather(gain_cols, "tensor", axis=1, tiled=True),
     )
     values = gathered.astype(jnp.float32)

time: 732 us -> 896 us (1.22)
  blocking collectives: 46.2 us -> 325 us
  waiting for transfers between devices: 588 us -> 452 us
  starting transfers between devices: 5.37 us -> 16.9 us
    all_to_all x0 -> x1, blocking collectives: none -> 147 us  [lax.all_to_all(jnp.stack(lax.axis_size(chip_axis) * [field_in]), axis_nam...]
    all_gather x2 -> x0, waiting for transfers between devices: 132 us -> none  [project(): lax.all_gather(stream, 'tensor', axis=2, tiled=True)]
    all_gather x1, blocking collectives: 46.2 us -> 178 us  [project(): lax.all_gather(gain_cols, 'tensor', axis=1, tiled=True)]
    all_to_all x0 -> x1, starting transfers between devices: none -> 11.7 us  [lax.all_to_all(jnp.stack(lax.axis_size(chip_axis) * [field_in]), axis_nam...]
  transfers between devices with their start and end apart: 9 -> 8, of which waited for: 9 -> 7; matrix products, arithmetic and copies ran while one was open for 1% -> 1% of each run, Pallas kernels for 0% -> 0%
where the time goes in v1:
time: 896 us
  waiting for transfers between devices  452 us (50%)
  blocking collectives  325 us (36%)
  other arithmetic  37.2 us (4%)
  matrix products  21.5 us (2%)
  local copies, waits for them, and re-layouts  19.8 us (2%)
  starting transfers between devices  16.9 us (2%)
  between operations  13.7 us (2%)
  loops' own time  9.56 us (1%)
    reduce_scatter x2, waiting for transfers between devices, mixing(): lax.psum_scatter(partial_terms.astype(jnp.bfloat16), 'tensor', scatter_di...  442 us
    all_gather x1, blocking collectives, project(): lax.all_gather(gain_cols, 'tensor', axis=1, tiled=True)  178 us
    all_to_all x1, blocking collectives, lax.all_to_all(jnp.stack(lax.axis_size(chip_axis) * [field_in]), axis_nam...  147 us
    add x256, other arithmetic, add_tap(): return running + long_taps[tap_index] * shifted  20.9 us
  transfers between devices with their start and end apart: 8, of which 7 were waited for; matrix products, arithmetic and copies ran while one was open for 1% of the time, Pallas kernels for 0%

profile of v1, /device:TPU:4, one launch (start us, length us, event | category | flops | bytes accessed | tf_op | source)
XLA Modules:
  0.0 895.8 jit_solution(12490926454951824374)
XLA Ops:
  6.5 1.4 fusion.10
  8.0 3.4 stack.10
  11.3 11.7 %all-to-all-start = ((bf16[32,2,192,256]{3,2,1,0:T(8,128)(2,1)}), bf16[32,2,192,256]{3,2,1,0:T(8,128)(2,1)}, u32[]{:S(2)}, u32[]{:S(2)}) async-start(bf16[32,2,192,256]{3,2,1,0:T(8,128)(2,1)} %stack.10), calls=%async_computation | async-start | bytes 12582912 | tf_op jit(solution)/shard_map/all_to_all | solution.py:14
  23.1 177.7 %all_gather.4 = bf16[1,8192]{1,0:T(2,128)(2,1)S(1)} all-gather(bf16[1,256]{1,0:T(2,128)(2,1)S(1)} %copy-done.4), channel_id=1, replica_groups=mesh['pipe'=2,'seq'=4,'tensor'=32] {'tensor'}, dimensions={1}, use_global_device_ids=true | all-gather | bytes 16896 | tf_op jit(solution)/shard_map/all_gather | solution.py:39
  201.0 8.8 copy.16
  209.8 4.3 fusion
  214.1 4.9 fusion.7
  219.1 3.5 copy.24
  222.5 5.6 convolution_convert_fusion.3
  228.1 1.3 collective-permute-start
  230.1 1.7 collective-permute-done
  231.8 2.8 collective-permute-done.1
  234.9 16.4 %while.32 = (s32[]{:T(128)}, f32[2,192,128]{2,1,0:T(8,128)S(1)}, f32[128,128]{1,0:T(8,128)S(1)}, f32[2,319,128]{2,1,0:T(8,128)S(1)}, s32[]{:T(128)}, /*index=5*/s32[]{:T(128)}, s32[]{:T(128)}, s32[]{:T(128)}) while((s32[]{:T(128)}, f32[2,192,128]{2,1,0:T(8,128)S(1)}, f32[128,128]{1,0:T(8,128)S(1)}, f32[2,319,128]{2,1,0:T(8,128)S(1)}, ...), condition=%wide.region_2.3_spmd.clone, body=%wide.region_1.2_spmd.clone.sunk | while | flops 147463 | bytes 591509 | solution.py:80
  251.4 4.5 convolution_convert_fusion.1
  255.9 221.1 %reduce-scatter.3.cloned.1.call-done = bf16[2,192,256]{2,1,0:T(8,128)(2,1)} async-done(((bf16[2,192,8192]{2,1,0:T(8,128)(2,1)}), bf16[2,192,256]{2,1,0:T(8,128)(2,1)}) %reduce-scatter.3.cloned.1.call-update) | async-done | bytes 196624 | tf_op jit(solution)/shard_map/reduce_scatter | solution.py:83
  477.0 1.0 add_convert_fusion.1
  478.0 1.3 collective-permute-start.2
  479.3 1.0 collective-permute-done.2
  480.4 0.7 stack.12
  481.1 147.5 %all_to_all.10 = bf16[32,2,192,256]{3,2,1,0:T(8,128)(2,1)S(1)} all-to-all(bf16[32,2,192,256]{3,2,1,0:T(8,128)(2,1)S(1)} %stack.12), channel_id=1, replica_groups=mesh['pipe'=2,'seq'=4,'tensor'=32] {'tensor'}, dimensions={0} | all-to-all | bytes 12582912 | tf_op jit(solution)/shard_map/all_to_all | solution.py:14
  628.6 1.3 fusion.3
  629.9 2.3 fusion.6
  632.2 0.8 copy.25
  633.1 5.6 convolution_convert_fusion.2
  638.6 1.3 collective-permute-start.3
  640.6 1.7 collective-permute-done.3
  642.4 2.8 collective-permute-done.4
  645.5 16.4 %while.33 = (s32[]{:T(128)}, f32[2,192,128]{2,1,0:T(8,128)S(1)}, f32[128,128]{1,0:T(8,128)S(1)}, f32[2,319,128]{2,1,0:T(8,128)S(1)}, s32[]{:T(128)}, /*index=5*/s32[]{:T(128)}, s32[]{:T(128)}, s32[]{:T(128)}) while((s32[]{:T(128)}, f32[2,192,128]{2,1,0:T(8,128)S(1)}, f32[128,128]{1,0:T(8,128)S(1)}, f32[2,319,128]{2,1,0:T(8,128)S(1)}, ...), condition=%wide.region_6.7_spmd.clone, body=%wide.region_5.6_spmd.clone.sunk | while | flops 147463 | bytes 591509 | solution.py:80
  661.9 4.5 convolution_convert_fusion
  666.4 220.8 %reduce-scatter.5.cloned.1.call-done = bf16[2,192,256]{2,1,0:T(8,128)(2,1)} async-done(((bf16[2,192,8192]{2,1,0:T(8,128)(2,1)}), bf16[2,192,256]{2,1,0:T(8,128)(2,1)}) %reduce-scatter.5.cloned.1.call-update) | async-done | bytes 196624 | tf_op jit(solution)/shard_map/reduce_scatter | solution.py:83
  887.2 1.0 fusion.17
  888.2 0.8 fusion.18
  (567 shorter events, 25.6 us)
Async XLA Ops:
  6.5 244.9 %copy-start = (bf16[1,128,8192]{2,1,0:T(8,128)(2,1)S(1)}, bf16[1,128,8192]{2,1,0:T(8,128)(2,1)}, u32[]{:S(2)}) copy-start(bf16[1,128,8192]{2,1,0:T(8,128)(2,1)} %param.18) | copy-start | bytes 6291460
  11.3 11.8 %copy-start.4 = (bf16[1,256]{1,0:T(2,128)(2,1)S(1)}, bf16[1,256]{1,0:T(2,128)(2,1)}, u32[]{:S(2)}) copy-start(bf16[1,256]{1,0:T(2,128)(2,1)} %param.19) | copy-start | bytes 1540
  11.3 198.5 %all-to-all-start = ((bf16[32,2,192,256]{3,2,1,0:T(8,128)(2,1)}), bf16[32,2,192,256]{3,2,1,0:T(8,128)(2,1)}, u32[]{:S(2)}, u32[]{:S(2)}) async-start(bf16[32,2,192,256]{3,2,1,0:T(8,128)(2,1)} %stack.10), calls=%async_computation | async-start | bytes 12582912 | tf_op jit(solution)/shard_map/all_to_all | solution.py:14
  23.1 454.0 %reduce-scatter.3.cloned.1.call-start = ((), (), s32[]{:S(2)}) async-start(), calls=%async_computation.4 | async-start | bytes 6488064 | tf_op jit(solution)/shard_map/reduce_scatter | solution.py:83
  201.0 8.8 copy-start.2
  201.0 8.8 copy-start.1
  201.0 8.8 copy-start.3
  209.8 12.7 %slice-start = ((s8[6291456]{0:T(1024)(128)(4,1)}), s8[4194304]{0:T(1024)(128)(4,1)S(1)}, s32[]{:S(2)}) async-start(s8[6291456]{0:T(1024)(128)(4,1)} %bitcast.46), calls=%async_computation.6 | async-start | bytes 8388608
  214.1 8.4 slice-start.1
  228.1 3.6 collective-permute-start
  229.5 5.1 collective-permute-start.1
  255.9 631.3 %reduce-scatter.5.cloned.1.call-start = ((), (), s32[]{:S(2)}) async-start(), calls=%async_computation.5 | async-start | bytes 6488064 | tf_op jit(solution)/shard_map/reduce_scatter | solution.py:83
  478.0 2.4 collective-permute-start.2
  638.6 3.7 collective-permute-start.3
  640.0 5.1 collective-permute-start.4
Sparse Core Ops, SparseCore 0:
  256.0 220.9 reduce-scatter.2
  666.5 220.6 reduce-scatter.4
